TPU v7x, 32 devices: a whole 2x2x4 slice. The times are simulated.
32 devices in a mesh: leaf: 8 (over z, y), blk: 4 (over x, core).
Axes of the slice: x: 2, y: 2, z: 4, core: 2. Of those that a mesh axis runs over, the one named last changes fastest.
Arguments:
- parent_inverse: bfloat16 [8, 512, 512], P('leaf', None, 'blk'), as said below
- leaf_inverse: bfloat16 [112, 512, 512], P('leaf', 'blk'), as said below
- coupling: bfloat16 [112, 512, 512], P('leaf', 'blk'), may hold values from -0.25 to 0.25
- sensitivity: bfloat16 [112, 512, 512], P('leaf', 'blk'), may hold values from -0.25 to 0.25
- parent_of: int32 [112, 1], P('leaf'), may hold values from 0 to 7
- leaf_field: bfloat16 [112, 512], P('leaf'), may hold values from -6 to 6
- parent_field: bfloat16 [8, 512], P('leaf', 'blk'), may hold values from -6 to 6
Outputs:
- leaf_grad: float32 [112, 512], P('leaf', 'blk')
- coupling_grad: float32 [8, 512], P('leaf', 'blk')
Inputs may be any that keep to these rules, and one draw needn't show every extreme that they name: `parent_of`: every one of the 8 separator supernodes is the parent of at least one leaf. `parent_inverse`: lower triangular with a positive diagonal. `leaf_inverse`: lower triangular with a positive diagonal.
All inputs are finite; a program needn't handle non-finite values.
Results may differ from a plain program's by a relative error of at most 0.0006.
Values may be sent and summed in bfloat16 or wider, within the bound.
No kernel may reach another device: no remote copies, remote signals or barrier semaphores. Data moves between devices by JAX's collectives and lax.ppermute only.
A program may use at most 128 MiB of HBM per device.

v0:
```python
import jax
import jax.numpy as jnp
from jax import lax
from jax.sharding import PartitionSpec as P


def body(parent_inverse, leaf_inverse, coupling, sensitivity, parent_of, leaf_field, parent_field):
    count = coupling.shape[0]
    share = coupling.shape[1]
    width = coupling.shape[2]
    offset = lax.axis_index("blk") * share
    cov_rows = jnp.einsum(
        "pkr,pkc->prc",
        parent_inverse,
        lax.all_gather(parent_inverse, "blk", axis=2, tiled=True),
        preferred_element_type=jnp.float32,
    ).astype(jnp.bfloat16)
    parent_ids = parent_of[:, 0]
    initial = (
        jnp.zeros((count, share, width), jnp.bfloat16),
        jnp.zeros((count, share), jnp.bfloat16),
    )
    pieces = (
        lax.all_gather(cov_rows, "leaf", axis=0, tiled=True),
        lax.all_gather(parent_field, "leaf", axis=0, tiled=True),
    )
    number = pieces[0].shape[0]
    inside = (parent_ids >= 0) & (parent_ids < number)
    position = jnp.clip(parent_ids, 0, number - 1)
    taken_cov = jnp.take(pieces[0], position, axis=0)
    taken_field = jnp.take(pieces[1], position, axis=0)
    chosen_cov = jnp.where(inside[:, None, None], taken_cov, initial[0])
    chosen_field = jnp.where(inside[:, None], taken_field, initial[1])
    panel = coupling
    mixed = jnp.einsum(
        "lik,lkc->lic",
        panel,
        lax.all_gather(leaf_inverse, "blk", axis=1, tiled=True),
        preferred_element_type=jnp.float32,
    ).astype(jnp.bfloat16)
    cross = jnp.zeros((count, share, width), jnp.float32) - jnp.einsum(
        "lrk,lkc->lrc",
        chosen_cov,
        lax.all_gather(mixed, "blk", axis=1, tiled=True),
        preferred_element_type=jnp.float32,
    )
    cross_half = cross.astype(jnp.bfloat16)
    panel = coupling
    update = lax.psum_scatter(
        jnp.einsum("lik,lia->kla", panel, cross_half, preferred_element_type=jnp.float32),
        "blk",
        scatter_dimension=0,
        tiled=True,
    )
    factor = leaf_inverse.astype(jnp.float32)
    partial_diag = jnp.sum(factor * factor, 1) - jnp.einsum(
        "lka,kla->la", factor, update, precision=lax.Precision.HIGHEST
    )
    diagonal = lax.psum_scatter(partial_diag, "blk", scatter_dimension=1, tiled=True)
    value = lax.dynamic_slice_in_dim(leaf_field, offset, share, 1).astype(jnp.float32)
    leaf_grad = 0.5 * (diagonal - value * value)
    returned = jnp.sum(sensitivity.astype(jnp.float32) * cross, 2) - chosen_field.astype(
        jnp.float32
    ) * jnp.einsum("lab,lb->la", sensitivity, leaf_field, preferred_element_type=jnp.float32)
    parent_total = lax.axis_size("leaf")
    owners = (
        parent_ids[:, None] == lax.broadcasted_iota(jnp.int32, (count, parent_total), 1)
    ).astype(jnp.float32)
    spread = jnp.einsum("lp,la->pa", owners, returned, precision=lax.Precision.HIGHEST)
    coupling_grad = lax.psum_scatter(spread, "leaf", scatter_dimension=0, tiled=True)
    return (leaf_grad, coupling_grad)


def solution(mesh):
    in_specs = (
        P("leaf", None, "blk"),
        P("leaf", "blk", None),
        P("leaf", "blk", None),
        P("leaf", "blk", None),
        P("leaf", None),
        P("leaf", None),
        P("leaf", "blk"),
    )
    out_specs = (P("leaf", "blk"), P("leaf", "blk"))
    return jax.shard_map(body, mesh=mesh, in_specs=in_specs, out_specs=out_specs, check_vma=False)
```

profile of v0, /device:TPU:0, one launch (start us, length us, event | category | flops | bytes accessed | tf_op | source)
XLA Modules:
  0.0 319.3 jit_solution(10498825598781214529)
XLA Ops:
  7.2 0.7 all-gather.6.cloned.1.call-update
  8.2 8.6 %all_gather.15 = bf16[1,512,512]{2,1,0:T(8,128)(2,1)S(1)} all-gather(bf16[1,512,128]{2,1,0:T(8,128)(2,1)S(1)} %copy-done.2), channel_id=1, replica_groups=mesh['leaf'=8,'blk'=4] {'blk'}, dimensions={2}, use_global_device_ids=true | all-gather | bytes 655360 | tf_op jit(solution)/shard_map/all_gather | solution.py:15
  16.9 0.9 convolution_convert_fusion.1
  17.8 46.8 %all-gather.6.cloned.1.call-done = bf16[14,512,512]{2,1,0:T(8,128)(2,1)} async-done(((bf16[14,128,512]{2,1,0:T(8,128)(2,1)}), bf16[14,512,512]{2,1,0:T(8,128)(2,1)}) %all-gather.6.cloned.1.call-update) | async-done | bytes 7340048 | tf_op jit(solution)/shard_map/all_gather | solution.py:38
  64.7 5.5 %convolution_convert_fusion = bf16[14,128,512]{2,1,0:T(8,128)(2,1)} fusion(bf16[14,128,512]{2,1,0:T(8,128)(2,1)S(1)} %copy-done, bf16[14,512,512]{2,1,0:T(8,128)(2,1)} %all-gather.6.cloned.1.call-done), kind=kOutput, calls=%fused_computation.13 | convolution fusion | flops 940441600 | bytes 11010048 | tf_op jit(solution)/shard_map/lik,lkc->lic/dot_general | solution.py:35
  70.3 0.6 copy-done.5
  70.9 36.3 %all-gather.10.cloned.1.call-done = bf16[1024,512]{1,0:T(8,128)(2,1)} async-done(((bf16[128,512]{1,0:T(8,128)(2,1)}), bf16[1024,512]{1,0:T(8,128)(2,1)}) %all-gather.10.cloned.1.call-update) | async-done | bytes 1048592 | tf_op jit(solution)/shard_map/all_gather | solution.py:24
  107.2 3.2 gather_fusion
  110.4 49.5 %all-gather.8.cloned.1.call-done = bf16[14,512,512]{2,1,0:T(8,128)(2,1)} async-done(((bf16[14,128,512]{2,1,0:T(8,128)(2,1)}), bf16[14,512,512]{2,1,0:T(8,128)(2,1)}) %all-gather.8.cloned.1.call-update) | async-done | bytes 7340048 | tf_op jit(solution)/shard_map/all_gather | solution.py:44
  159.8 5.4 %multiply_reduce_fusion.1 = (f32[14,128]{1,0:T(8,128)S(1)}, f32[14,128,512]{2,1,0:T(8,128)S(1)}) fusion(bf16[14,128,512]{2,1,0:T(8,128)(2,1)} %param.10, bf16[14,512,512]{2,1,0:T(8,128)(2,1)} %all-gather.8.cloned.1.call-done, bf16[14,128,512]{2,1,0:T(8,128)(2,1)} %gather_fusion, pred[14]{0:T(512)(128)(4,1)S(1)} %get-tuple-element.3, ...), kind=kOutput, calls=%fused_computation.4 | convolution fusion | flops 945027328 | bytes 14687260 | tf_op jit(solution)/shard_map/lrk,lkc->lrc/dot_general | solution.py:41
  165.2 7.3 %convolution_bitcast_fusion = f32[512,14,512]{0,2,1:T(8,128)} fusion(bf16[14,128,512]{2,1,0:T(8,128)(2,1)S(1)} %copy-done, f32[14,128,512]{2,1,0:T(8,128)S(1)} %get-tuple-element.5), kind=kOutput, calls=%fused_computation.2 | convolution fusion | flops 941359104 | bytes 20185088 | tf_op jit(solution)/shard_map/lik,lia->kla/dot_general | solution.py:50
  173.2 20.5 %all-gather.1 = bf16[8,1,128]{2,1,0:T(2,128)(2,1)S(1)} all-gather(bf16[1,1,128]{2,1,0:T(2,128)(2,1)S(1)} %bitcast.40), channel_id=1, replica_groups=mesh['leaf'=8,'blk'=4] {'leaf'}, dimensions={0}, use_global_device_ids=true | all-gather | bytes 2304 | tf_op jit(solution)/shard_map/all_gather | solution.py:25
  193.7 0.6 gather_fusion.1
  194.3 0.6 dynamic-slice
  194.9 1.9 multiply_reduce_fusion.2
  196.8 0.6 fusion.10
  197.7 17.3 %all-reduce = f32[8,128]{1,0:T(8,128)S(1)} all-reduce(f32[8,128]{1,0:T(8,128)S(1)} %fusion.13), channel_id=5, replica_groups=mesh['leaf'=8,'blk'=4] {'leaf'}, use_global_device_ids=true, to_apply=%region_4.5.clone | all-reduce | flops 1024 | bytes 8192
  214.9 67.8 %reduce-scatter.3.cloned.1.call-done = f32[128,14,512]{0,2,1:T(8,128)} async-done(((f32[512,14,512]{0,2,1:T(8,128)}), f32[128,14,512]{0,2,1:T(8,128)}) %reduce-scatter.3.cloned.1.call-update) | async-done | bytes 3670032 | tf_op jit(solution)/shard_map/reduce_scatter | solution.py:49
  282.8 5.1 %copy.17 = f32[14,512,128]{1,2,0:T(8,128)} copy(f32[14,512,128]{2,1,0:T(8,128)} %bitcast.36) | data formatting | bytes 7340032
  287.9 3.2 %multiply_reduce_fusion = f32[14,512]{1,0:T(8,128)S(1)} fusion(f32[14,512,128]{1,2,0:T(8,128)} %copy.17, bf16[14,128,512]{2,1,0:T(8,128)(2,1)} %param.8), kind=kLoop, calls=%fused_computation.3 | loop fusion | flops 2745344 | bytes 5533696 | tf_op jit(solution)/shard_map/lka,kla->la/dot_general | solution.py:56
  291.1 0.6 sub.13
  291.8 1.2 constant_dynamic-slice_fusion
  293.0 18.5 %reduce-scatter.5.cloned.1.call-done = f32[14,128]{1,0:T(8,128)} async-done(((f32[14,512]{1,0:T(8,128)}), f32[14,128]{1,0:T(8,128)}) %reduce-scatter.5.cloned.1.call-update) | async-done | bytes 7184 | tf_op jit(solution)/shard_map/reduce_scatter | solution.py:59
  311.5 1.3 subtract_multiply_fusion
  (28 shorter events, 1.4 us)
Async XLA Ops:
  7.2 57.5 %copy-start = (bf16[14,128,512]{2,1,0:T(8,128)(2,1)S(1)}, bf16[14,128,512]{2,1,0:T(8,128)(2,1)}, u32[]{:S(2)}) copy-start(bf16[14,128,512]{2,1,0:T(8,128)(2,1)} %param.9) | copy-start | bytes 5505028
  7.2 1.0 copy-start.2
  7.2 57.5 %all-gather.6.cloned.1.call-start = ((), (), s32[]{:S(2)}) async-start(), calls=%async_computation.2 | async-start | bytes 9175040 | tf_op jit(solution)/shard_map/all_gather | solution.py:38
  7.9 99.3 %all-gather.10.cloned.1.call-start = ((), (), s32[]{:S(2)}) async-start(), calls=%async_computation.6 | async-start | bytes 1179648 | tf_op jit(solution)/shard_map/all_gather | solution.py:24
  17.8 142.0 %all-gather.8.cloned.1.call-start = ((), (), s32[]{:S(2)}) async-start(), calls=%async_computation.3 | async-start | bytes 9175040 | tf_op jit(solution)/shard_map/all_gather | solution.py:44
  70.2 0.7 copy-start.5
  70.2 212.6 %reduce-scatter.3.cloned.1.call-start = ((), (), s32[]{:S(2)}) async-start(), calls=%async_computation.4 | async-start | bytes 18350080 | tf_op jit(solution)/shard_map/reduce_scatter | solution.py:49
  172.6 0.7 copy-start.4
  172.6 21.7 %copy-start.6 = (u32[32]{0:T(128)S(1)}, u32[32]{0:T(128)}, u32[]{:S(2)}) copy-start(u32[32]{0:T(128)} %constant.58) | copy-start | bytes 388
  172.6 24.2 %copy-start.3 = (bf16[14,512]{1,0:T(8,128)(2,1)S(1)}, bf16[14,512]{1,0:T(8,128)(2,1)}, u32[]{:S(2)}) copy-start(bf16[14,512]{1,0:T(8,128)(2,1)} %param.12) | copy-start | bytes 43012
  172.6 138.9 %reduce-scatter.5.cloned.1.call-start = ((), (), s32[]{:S(2)}) async-start(), calls=%async_computation.5 | async-start | bytes 40960 | tf_op jit(solution)/shard_map/reduce_scatter | solution.py:59
  194.3 2.5 copy-start.1
Sparse Core Ops, SparseCore 0:
  9.6 55.0 all-gather.5
  66.8 40.3 all-gather.9
  108.8 51.0 all-gather.7
  172.7 110.0 reduce-scatter.2
  291.9 19.5 reduce-scatter.4
where the time goes:
time: 320 us; the launch traced here: 319 us
  waiting for transfers between devices  220 us (69%)
  blocking collectives  46.4 us (14%)
  matrix products  20 us (6%)
  between operations  13.9 us (4%)
  local copies, waits for them, and re-layouts  12 us (4%)
  other arithmetic  7.09 us (2%)
    reduce_scatter x1, waiting for transfers between devices, body(): lax.psum_scatter(jnp.einsum('lik,lia->kla', panel, cross_half, preferred_...  67.8 us
    all_gather x1, waiting for transfers between devices, body(): lax.all_gather(mixed, 'blk', axis=1, tiled=True)  49.5 us
    all_gather x1, waiting for transfers between devices, body(): lax.all_gather(leaf_inverse, 'blk', axis=1, tiled=True)  46.8 us
    all_gather x1, waiting for transfers between devices, body(): lax.all_gather(cov_rows, 'leaf', axis=0, tiled=True)  36.3 us
    all_gather x1, blocking collectives, body(): lax.all_gather(parent_field, 'leaf', axis=0, tiled=True)  20.5 us
    reduce_scatter x1, waiting for transfers between devices, body(): lax.psum_scatter(partial_diag, 'blk', scatter_dimension=1, tiled=True)  18.5 us
    unnamed x1, blocking collectives  17.3 us
    all_gather x1, blocking collectives, body(): lax.all_gather(parent_inverse, 'blk', axis=2, tiled=True)  8.63 us
  transfers between devices with their start and end apart: 5, of which 5 were waited for; matrix products, arithmetic and copies ran while one was open for 5% of the time, Pallas kernels for 0%

commit v1 on v0

--- a/solution.py
+++ b/solution.py
@@ -2,6 +2,22 @@
 import jax.numpy as jnp
 from jax import lax
 from jax.sharding import PartitionSpec as P
+
+
+def product_in_turn(x, axis, dim, term):
+    devices, place, rows = (lax.axis_size(axis), lax.axis_index(axis), x.shape[dim])
+    right = [(i, (i + 1) % devices) for i in range(devices)]
+    backward = [(i, (i - 1) % devices) for i in range(devices)]
+    half = devices // 2
+    from_left = from_right = x
+    total = term(x, place * rows)
+    for step in range(1, half + 1):
+        from_left = lax.ppermute(from_left, axis, right)
+        if step < devices - half:
+            from_right = lax.ppermute(from_right, axis, backward)
+            total = total + term(from_right, (place + step) % devices * rows)
+        total = total + term(from_left, (place - step) % devices * rows)
+    return total
 
 
 def body(parent_inverse, leaf_inverse, coupling, sensitivity, parent_of, leaf_field, parent_field):
@@ -38,11 +54,16 @@
         lax.all_gather(leaf_inverse, "blk", axis=1, tiled=True),
         preferred_element_type=jnp.float32,
     ).astype(jnp.bfloat16)
-    cross = jnp.zeros((count, share, width), jnp.float32) - jnp.einsum(
-        "lrk,lkc->lrc",
-        chosen_cov,
-        lax.all_gather(mixed, "blk", axis=1, tiled=True),
-        preferred_element_type=jnp.float32,
+    cross = jnp.zeros((count, share, width), jnp.float32) - product_in_turn(
+        mixed,
+        "blk",
+        1,
+        lambda own_block, start: jnp.einsum(
+            "lrk,lkc->lrc",
+            lax.dynamic_slice_in_dim(chosen_cov, start, own_block.shape[1], axis=2),
+            own_block,
+            preferred_element_type=jnp.float32,
+        ),
     )
     cross_half = cross.astype(jnp.bfloat16)
     panel = coupling

time: 320 us -> 307 us (0.959)
  waiting for transfers between devices: 220 us -> 184 us
  blocking collectives: 46.4 us -> 62.1 us
  matrix products: 20 us -> 23.9 us
    all_gather x1 -> x0, waiting for transfers between devices: 49.5 us -> none  [body(): lax.all_gather(mixed, 'blk', axis=1, tiled=True)]
    all_gather x1, blocking collectives: 8.63 us -> 26 us  [body(): lax.all_gather(parent_inverse, 'blk', axis=2, tiled=True)]
    all_gather x1, waiting for transfers between devices: 46.8 us -> 56.6 us  [body(): lax.all_gather(leaf_inverse, 'blk', axis=1, tiled=True)]
    dot_general x1 -> x4, matrix products: 5.4 us -> 9.33 us  [body(): jnp.einsum('lrk,lkc->lrc', lax.dynamic_slice_in_dim(chosen_cov, start, ow...]
    all_gather x1, waiting for transfers between devices: 36.3 us -> 39.7 us  [body(): lax.all_gather(cov_rows, 'leaf', axis=0, tiled=True)]
    unnamed x18 -> x20, local copies, waits for them, and re-layouts: 8.29 us -> 7.47 us
  transfers between devices with their start and end apart: 5 -> 7, of which waited for: 5 -> 4; matrix products, arithmetic and copies ran while one was open for 5% -> 6% of each run, Pallas kernels for 0% -> 0%
where the time goes in v1:
time: 307 us; the launch traced here: 306 us
  waiting for transfers between devices  184 us (60%)
  blocking collectives  62.1 us (20%)
  matrix products  23.9 us (8%)
  between operations  15.3 us (5%)
  local copies, waits for them, and re-layouts  11.2 us (4%)
  other arithmetic  8.85 us (3%)
    reduce_scatter x1, waiting for transfers between devices, body(): lax.psum_scatter(jnp.einsum('lik,lia->kla', panel, cross_half, preferred_...  68.2 us
    all_gather x1, waiting for transfers between devices, body(): lax.all_gather(leaf_inverse, 'blk', axis=1, tiled=True)  56.6 us
    all_gather x1, waiting for transfers between devices, body(): lax.all_gather(cov_rows, 'leaf', axis=0, tiled=True)  39.7 us
    all_gather x1, blocking collectives, body(): lax.all_gather(parent_inverse, 'blk', axis=2, tiled=True)  26 us
    reduce_scatter x1, waiting for transfers between devices, body(): lax.psum_scatter(partial_diag, 'blk', scatter_dimension=1, tiled=True)  18.5 us
    all_gather x1, blocking collectives, body(): lax.all_gather(parent_field, 'leaf', axis=0, tiled=True)  18.3 us
    unnamed x1, blocking collectives  17.8 us
    dot_general x4, matrix products, body(): jnp.einsum('lrk,lkc->lrc', lax.dynamic_slice_in_dim(chosen_cov, start, ow...  9.33 us
  transfers between devices with their start and end apart: 7, of which 4 were waited for; matrix products, arithmetic and copies ran while one was open for 6% of the time, Pallas kernels for 0%

profile of v1, /device:TPU:0, one launch (start us, length us, event | category | flops | bytes accessed | tf_op | source)
XLA Modules:
  0.0 306.2 jit_solution(16177981464992754310)
XLA Ops:
  8.1 0.7 all-gather.5.cloned.1.call-update
  8.8 56.6 %all-gather.5.cloned.1.call-done = bf16[14,512,512]{2,1,0:T(8,128)(2,1)} async-done(((bf16[14,128,512]{2,1,0:T(8,128)(2,1)}), bf16[14,512,512]{2,1,0:T(8,128)(2,1)}) %all-gather.5.cloned.1.call-update) | async-done | bytes 7340048 | tf_op jit(solution)/shard_map/all_gather | solution.py:54
  65.4 5.5 %convolution_convert_fusion = bf16[14,128,512]{2,1,0:T(8,128)(2,1)} fusion(bf16[14,128,512]{2,1,0:T(8,128)(2,1)S(1)} %copy-done, bf16[14,512,512]{2,1,0:T(8,128)(2,1)} %all-gather.5.cloned.1.call-done), kind=kOutput, calls=%fused_computation.9 | convolution fusion | flops 940441600 | bytes 11010048 | tf_op jit(solution)/shard_map/lik,lkc->lic/dot_general | solution.py:51
  71.2 26.0 %all_gather.12 = bf16[1,512,512]{2,1,0:T(8,128)(2,1)S(1)} all-gather(bf16[1,512,128]{2,1,0:T(8,128)(2,1)S(1)} %copy-done.3), channel_id=1, replica_groups=mesh['leaf'=8,'blk'=4] {'blk'}, dimensions={2}, use_global_device_ids=true | all-gather | bytes 655360 | tf_op jit(solution)/shard_map/all_gather | solution.py:31
  97.2 0.9 convolution_convert_fusion.1
  98.8 39.7 %all-gather.7.cloned.1.call-done = bf16[1024,512]{1,0:T(8,128)(2,1)} async-done(((bf16[128,512]{1,0:T(8,128)(2,1)}), bf16[1024,512]{1,0:T(8,128)(2,1)}) %all-gather.7.cloned.1.call-update) | async-done | bytes 1048592 | tf_op jit(solution)/shard_map/all_gather | solution.py:40
  138.5 3.2 %gather_fusion = bf16[14,128,512]{2,1,0:T(8,128)(2,1)} fusion(bf16[8,128,512]{2,1,0:T(8,128)(2,1)} %bitcast.41, s32[1024]{0:T(1024)S(1)} %pad_clamp_fusion), kind=kCustom, calls=%fused_computation | custom fusion | bytes 3670072 | tf_op jit(solution)/shard_map/jit(_take)/gather | solution.py:46
  141.7 1.8 select_select_fusion
  143.5 2.1 fusion.7
  145.6 2.1 fusion.3
  147.8 2.3 fusion.5
  150.0 2.8 multiply_reduce_fusion.1
  152.9 7.3 %convolution_bitcast_fusion = f32[512,14,512]{0,2,1:T(8,128)} fusion(bf16[14,128,512]{2,1,0:T(8,128)(2,1)S(1)} %copy-done, bf16[14,128,512]{2,1,0:T(8,128)(2,1)S(1)} %get-tuple-element.5), kind=kOutput, calls=%fused_computation.2 | convolution fusion | flops 939524096 | bytes 18350080 | tf_op jit(solution)/shard_map/lik,lia->kla/dot_general | solution.py:71
  160.8 18.3 %all-gather.1 = bf16[8,1,128]{2,1,0:T(2,128)(2,1)S(1)} all-gather(bf16[1,1,128]{2,1,0:T(2,128)(2,1)S(1)} %bitcast.44), channel_id=1, replica_groups=mesh['leaf'=8,'blk'=4] {'leaf'}, dimensions={0}, use_global_device_ids=true | all-gather | bytes 2304 | tf_op jit(solution)/shard_map/all_gather | solution.py:41
  179.7 0.6 dynamic-slice
  180.3 1.9 multiply_reduce_fusion.2
  183.1 17.8 %all-reduce = f32[8,128]{1,0:T(8,128)S(1)} all-reduce(f32[8,128]{1,0:T(8,128)S(1)} %fusion.13), channel_id=5, replica_groups=mesh['leaf'=8,'blk'=4] {'leaf'}, use_global_device_ids=true, to_apply=%region_4.5.clone | all-reduce | flops 1024 | bytes 8192
  200.9 68.2 %reduce-scatter.3.cloned.1.call-done = f32[128,14,512]{0,2,1:T(8,128)} async-done(((f32[512,14,512]{0,2,1:T(8,128)}), f32[128,14,512]{0,2,1:T(8,128)}) %reduce-scatter.3.cloned.1.call-update) | async-done | bytes 3670032 | tf_op jit(solution)/shard_map/reduce_scatter | solution.py:70
  269.1 5.1 %copy.17 = f32[14,512,128]{1,2,0:T(8,128)} copy(f32[14,512,128]{2,1,0:T(8,128)} %bitcast.40) | data formatting | bytes 7340032
  274.2 3.2 %multiply_reduce_fusion = f32[14,512]{1,0:T(8,128)S(1)} fusion(f32[14,512,128]{1,2,0:T(8,128)} %copy.17, bf16[14,128,512]{2,1,0:T(8,128)(2,1)} %param.8), kind=kLoop, calls=%fused_computation.3 | loop fusion | flops 2745344 | bytes 5533696 | tf_op jit(solution)/shard_map/lka,kla->la/dot_general | solution.py:77
  277.5 0.6 sub.21
  278.1 1.2 constant_dynamic-slice_fusion
  279.3 18.5 %reduce-scatter.5.cloned.1.call-done = f32[14,128]{1,0:T(8,128)} async-done(((f32[14,512]{1,0:T(8,128)}), f32[14,128]{1,0:T(8,128)}) %reduce-scatter.5.cloned.1.call-update) | async-done | bytes 7184 | tf_op jit(solution)/shard_map/reduce_scatter | solution.py:80
  297.8 1.3 subtract_multiply_fusion
  (37 shorter events, 3.1 us)
Async XLA Ops:
  8.0 57.5 %copy-start = (bf16[14,128,512]{2,1,0:T(8,128)(2,1)S(1)}, bf16[14,128,512]{2,1,0:T(8,128)(2,1)}, u32[]{:S(2)}) copy-start(bf16[14,128,512]{2,1,0:T(8,128)(2,1)} %param.9) | copy-start | bytes 5505028
  8.0 57.4 %all-gather.5.cloned.1.call-start = ((), (), s32[]{:S(2)}) async-start(), calls=%async_computation.2 | async-start | bytes 9175040 | tf_op jit(solution)/shard_map/all_gather | solution.py:54
  8.7 62.5 %copy-start.3 = (bf16[1,512,128]{2,1,0:T(8,128)(2,1)S(1)}, bf16[1,512,128]{2,1,0:T(8,128)(2,1)}, u32[]{:S(2)}) copy-start(bf16[1,512,128]{2,1,0:T(8,128)(2,1)} %param.7) | copy-start | bytes 393220
  8.8 89.6 %copy-start.6 = (s32[14,1]{0,1:T(1,128)S(1)}, s32[14,1]{0,1:T(1,128)}, u32[]{:S(2)}) copy-start(s32[14,1]{0,1:T(1,128)} %param.11) | copy-start | bytes 172
  8.8 129.8 %all-gather.7.cloned.1.call-start = ((), (), s32[]{:S(2)}) async-start(), calls=%async_computation.5 | async-start | bytes 1179648 | tf_op jit(solution)/shard_map/all_gather | solution.py:40
  71.0 27.4 %collective-permute-start.1 = (bf16[14,128,512]{2,1,0:T(8,128)(2,1)}, bf16[14,128,512]{2,1,0:T(8,128)(2,1)}, u32[]{:S(2)}, u32[]{:S(2)}) collective-permute-start(bf16[14,128,512]{2,1,0:T(8,128)(2,1)} %convolution_convert_fusion), channel_id=1, source_target_pairs={{0,1},{1,2},{2,3},{3,0},{4,5},{5,6},{6,7},{7,4},{8,9},{9,10},{10,1... | collective-permute-start | bytes 5505032 | tf_op jit(solution)/shard_map/ppermute | solution.py:15
  98.1 171.0 %reduce-scatter.3.cloned.1.call-start = ((), (), s32[]{:S(2)}) async-start(), calls=%async_computation.3 | async-start | bytes 18350080 | tf_op jit(solution)/shard_map/reduce_scatter | solution.py:70
  98.2 49.6 %collective-permute-start = (bf16[14,128,512]{2,1,0:T(8,128)(2,1)}, bf16[14,128,512]{2,1,0:T(8,128)(2,1)}, u32[]{:S(2)}, u32[]{:S(2)}) collective-permute-start(bf16[14,128,512]{2,1,0:T(8,128)(2,1)} %convolution_convert_fusion), channel_id=1, source_target_pairs={{0,3},{1,0},{2,1},{3,2},{4,7},{5,4},{6,5},{7,6},{8,11},{9,8},{10,9... | collective-permute-start | bytes 5505032 | tf_op jit(solution)/shard_map/ppermute | solution.py:17
  98.4 51.7 %collective-permute-start.2 = (bf16[14,128,512]{2,1,0:T(8,128)(2,1)}, bf16[14,128,512]{2,1,0:T(8,128)(2,1)}, u32[]{:S(2)}, u32[]{:S(2)}) collective-permute-start(bf16[14,128,512]{2,1,0:T(8,128)(2,1)} %collective-permute-done.1), channel_id=1, source_target_pairs={{0,1},{1,2},{2,3},{3,0},{4,5},{5,6},{6,7},{7,4},{8,9},{9,10},{10,1... | collective-permute-start | bytes 5505032 | tf_op jit(solution)/shard_map/ppermute | solution.py:15
  147.7 2.3 copy-start.1
  160.2 0.7 copy-start.5
  160.2 19.5 %copy-start.7 = (u32[32]{0:T(128)S(1)}, u32[32]{0:T(128)}, u32[]{:S(2)}) copy-start(u32[32]{0:T(128)} %constant.85) | copy-start | bytes 388
  160.2 22.0 %copy-start.4 = (bf16[14,512]{1,0:T(8,128)(2,1)S(1)}, bf16[14,512]{1,0:T(8,128)(2,1)}, u32[]{:S(2)}) copy-start(bf16[14,512]{1,0:T(8,128)(2,1)} %param.12) | copy-start | bytes 43012
  160.2 137.6 %reduce-scatter.5.cloned.1.call-start = ((), (), s32[]{:S(2)}) async-start(), calls=%async_computation.4 | async-start | bytes 40960 | tf_op jit(solution)/shard_map/reduce_scatter | solution.py:80
  179.7 2.5 copy-start.2
Sparse Core Ops, SparseCore 0:
  10.4 55.0 all-gather.4
  160.3 108.7 reduce-scatter.2
  278.2 19.5 reduce-scatter.4
Sparse Core Ops, SparseCore 1:
  98.2 40.3 all-gather.6
